TPU v7x, 32 devices: a whole 2x2x4 slice. The times are simulated.
32 devices in a mesh: seq: 8 (over y, x, core), head: 4 (over z).
Axes of the slice: x: 2, y: 2, z: 4, core: 2. Of those that a mesh axis runs over, the one named last changes fastest.
Arguments:
- queries: bfloat16 [4096, 64, 128], P(('seq', 'head')), may hold values from -36 to 36
- keys: bfloat16 [4096, 8, 128], P(('seq', 'head')), may hold values from -6 to 6
- values: bfloat16 [4096, 8, 128], P(('seq', 'head')), may hold values from -6 to 6
- output_gradient: bfloat16 [4096, 64, 128], P(('seq', 'head')), may hold values from -6 to 6
- global_blocks: int32 [2], replicated, may hold values from 0 to 31, as said below
- random_blocks: int32 [32, 3], replicated, may hold values from 0 to 31, as said below
Outputs:
- out: bfloat16 [4096, 64, 128], P(('seq', 'head'))
- grad_queries: bfloat16 [4096, 64, 128], P(('seq', 'head'))
- grad_keys: bfloat16 [4096, 8, 128], P(('seq', 'head'))
- grad_values: bfloat16 [4096, 8, 128], P(('seq', 'head'))
Inputs may be any that keep to these rules, and one draw needn't show every extreme that they name: `global_blocks`: the two blocks differ; one of them is the last block, 31. `random_blocks`: call 4 consecutive blocks starting at a multiple of 4 a group. The entries listed by a group's query blocks never lie in that group's own blocks, and at most 2 of them lie in any one other group; in every group some other group is hit exactly 2 times.
All inputs are finite; a program needn't handle non-finite values.
Results may differ from a plain program's by a relative error of at most 0.035.
Values may be sent and summed in bfloat16 or wider, within the bound.
No kernel may reach another device: no remote copies, remote signals or barrier semaphores. Data moves between devices by JAX's collectives and lax.ppermute only.
A program may use at most 128 MiB of HBM per device.

v0:
```python
import math
import jax
import jax.numpy as jnp
from jax import lax
from jax.sharding import PartitionSpec as P

BLOCK_TOKENS = 128


def padded(shard, sides, width):
    for axis, dim in sides:
        count, length = (lax.axis_size(axis), shard.shape[dim])
        up = [(i, (i + 1) % count) for i in range(count - 1)]
        down = [(j, i) for i, j in up]
        last = lax.slice_in_dim(shard, length - width, length, axis=dim)
        leading = lax.slice_in_dim(shard, 0, width, axis=dim)
        before = lax.ppermute(last, axis, up)
        after = lax.ppermute(leading, axis, down)
        shard = jnp.concatenate([before, shard, after], axis=dim)
    return shard


def from_root(block, axis, owner):
    block = jnp.where(lax.axis_index(axis) == owner, block, jnp.zeros_like(block))
    return lax.psum(block, axis)


def tree_sum(part, axis):
    count = lax.axis_size(axis)
    if count & count - 1:
        return lax.psum(part.astype(jnp.bfloat16), axis).astype(jnp.float32)
    stride = 1
    while stride < count:
        pairs = [(i, i ^ stride) for i in range(count)]
        other = lax.ppermute(part.astype(jnp.bfloat16), axis, pairs)
        part = part + other.astype(jnp.float32)
        stride *= 2
    return part


def head_exchange(array, split_axis, concat_axis):
    count = lax.axis_size("head")
    own = lax.axis_index("head")
    piece = array.shape[split_axis] // count
    received = []
    for shift in range(count):
        target = (own + shift) % count
        part = lax.dynamic_slice_in_dim(array, target * piece, piece, split_axis)
        if shift:
            pairs = [(i, (i + shift) % count) for i in range(count)]
            part = lax.ppermute(part, "head", pairs)
        received.append(part)
    order = (own - jnp.arange(count)) % count
    stacked = jnp.take(jnp.stack(received), order, axis=0)
    stacked = jnp.moveaxis(stacked, 0, concat_axis)
    shape = list(array.shape)
    shape[split_axis] = piece
    shape[concat_axis] *= count
    return stacked.reshape(shape)


def per_chunk(queries, keys, values, output_gradient, global_blocks, random_blocks, gate):
    query_loc, key_loc, value_loc, grad_loc = (
        lax.all_to_all(queries, "head", split_axis=1, concat_axis=0, tiled=True),
        lax.all_to_all(keys, "head", split_axis=1, concat_axis=0, tiled=True),
        lax.all_to_all(values, "head", split_axis=1, concat_axis=0, tiled=True),
        lax.all_to_all(output_gradient, "head", split_axis=1, concat_axis=0, tiled=True),
    )
    if gate is not None:
        (query_loc, grad_loc), gate = lax.optimization_barrier(((query_loc, grad_loc), gate))
    shard_len, heads_q, head_width = query_loc.shape
    heads_kv = key_loc.shape[1]
    heads_per_group = heads_q // heads_kv
    kv_width = heads_kv * head_width
    blocks = shard_len // BLOCK_TOKENS
    seq_count = lax.axis_size("seq")
    own_index = lax.axis_index("seq")
    block_total_count = seq_count * blocks
    capacity = (3 * blocks + seq_count - 2) // (seq_count - 1)
    entry_count = 3 * blocks
    score_scale = 1.0 / math.sqrt(head_width)
    kv_pair = jnp.stack(
        [key_loc.reshape(shard_len, kv_width), value_loc.reshape(shard_len, kv_width)]
    )
    extended = padded(kv_pair, (("seq", 1),), BLOCK_TOKENS)
    kv_tiles = kv_pair.reshape(2, blocks, BLOCK_TOKENS, kv_width).transpose(1, 0, 2, 3)
    global_owner = global_blocks // blocks
    global_offset = global_blocks % blocks
    own_global = (jnp.arange(blocks)[None, :] == global_offset[:, None]) & (
        global_owner == own_index
    )[:, None]
    all_entries = (
        random_blocks.reshape(seq_count, blocks, 3)
        .transpose(0, 2, 1)
        .reshape(seq_count, entry_count)
    )
    all_owner = all_entries // blocks
    entry_ids = jnp.arange(entry_count)
    entry_earlier = entry_ids[None, :] < entry_ids[:, None]
    all_rank = jnp.sum(
        (all_owner[:, :, None] == all_owner[:, None, :]) & entry_earlier[None], axis=2
    )
    my_entries = lax.dynamic_index_in_dim(all_entries, own_index, 0, keepdims=False)
    my_owner = lax.dynamic_index_in_dim(all_owner, own_index, 0, keepdims=False)
    my_rank = lax.dynamic_index_in_dim(all_rank, own_index, 0, keepdims=False)
    my_slot = my_owner * capacity + my_rank
    owned_here = (all_owner == own_index)[:, :, None] & (
        all_rank[:, :, None] == jnp.arange(capacity)[None, None, :]
    )
    offset_match = (all_entries % blocks)[:, :, None] == jnp.arange(blocks)[None, None, :]
    selector = jnp.einsum(
        "tec,teo->tco",
        owned_here.astype(jnp.bfloat16),
        offset_match.astype(jnp.bfloat16),
        preferred_element_type=jnp.float32,
    ).astype(jnp.bfloat16)
    everything = lax.all_gather(kv_pair, "seq", axis=1, tiled=True)
    tiled_all = everything.reshape(2, block_total_count, BLOCK_TOKENS, kv_width)
    random_tiles = jnp.take(tiled_all, my_entries, axis=1).transpose(1, 0, 2, 3)
    global_tiles = jnp.take(tiled_all, global_blocks, axis=1).transpose(1, 0, 2, 3)
    random_by_block = random_tiles.reshape(3, blocks, 2, BLOCK_TOKENS, kv_width).transpose(
        1, 0, 2, 3, 4
    )
    block_ids = own_index * blocks + jnp.arange(blocks)
    listed = jnp.concatenate(
        [
            jnp.stack([block_ids - 1, block_ids, block_ids + 1], axis=1),
            jnp.broadcast_to(global_blocks[None, :], (blocks, 2)),
            my_entries.reshape(3, blocks).T,
        ],
        axis=1,
    )
    inside = (listed >= 0) & (listed < block_total_count)
    tile_ids = jnp.arange(8)
    tile_earlier = tile_ids[None, :] < tile_ids[:, None]
    repeat = jnp.any((listed[:, :, None] == listed[:, None, :]) & tile_earlier[None], axis=2)
    live = inside & jnp.logical_not(repeat)

    def attend(unused_state, inputs):
        query_blk, grad_blk, random_blk, live_row, position = inputs
        near_tiles = lax.dynamic_slice_in_dim(
            extended, position * BLOCK_TOKENS, 3 * BLOCK_TOKENS, 1
        )
        near_tiles = near_tiles.reshape(2, 3, BLOCK_TOKENS, kv_width).transpose(1, 0, 2, 3)
        all_tiles = jnp.concatenate([near_tiles, global_tiles, random_blk], axis=0)
        key_t = all_tiles[:, 0].reshape(8, BLOCK_TOKENS, heads_kv, head_width)
        value_t = all_tiles[:, 1].reshape(8, BLOCK_TOKENS, heads_kv, head_width)
        query_grid = query_blk.reshape(BLOCK_TOKENS, heads_kv, heads_per_group, head_width)
        grad_grid = grad_blk.reshape(BLOCK_TOKENS, heads_kv, heads_per_group, head_width)
        scores = (
            jnp.einsum("qkgd,tbkd->kgqtb", query_grid, key_t, preferred_element_type=jnp.float32)
            * score_scale
        )
        scores = jnp.where(live_row[None, None, None, :, None], scores, -jnp.inf)
        row_max = jnp.max(scores, axis=(3, 4), keepdims=True)
        expo = jnp.exp(scores - row_max)
        attn_prob = expo / jnp.sum(expo, axis=(3, 4), keepdims=True)
        prob_low = attn_prob.astype(jnp.bfloat16)
        attended = jnp.einsum(
            "kgqtb,tbkd->qkgd", prob_low, value_t, preferred_element_type=jnp.float32
        )
        out_low = attended.astype(jnp.bfloat16)
        row_delta = jnp.sum(grad_grid.astype(jnp.float32) * out_low.astype(jnp.float32), axis=-1)
        grad_prob = jnp.einsum(
            "qkgd,tbkd->kgqtb", grad_grid, value_t, preferred_element_type=jnp.float32
        )
        grad_score = attn_prob * (
            grad_prob - jnp.transpose(row_delta, (1, 2, 0))[:, :, :, None, None]
        )
        score_low = grad_score.astype(jnp.bfloat16)
        query_grad = (
            jnp.einsum("kgqtb,tbkd->qkgd", score_low, key_t, preferred_element_type=jnp.float32)
            * score_scale
        )
        key_grad = (
            jnp.einsum(
                "kgqtb,qkgd->tbkd", score_low, query_grid, preferred_element_type=jnp.float32
            )
            * score_scale
        )
        value_grad = jnp.einsum(
            "kgqtb,qkgd->tbkd", prob_low, grad_grid, preferred_element_type=jnp.float32
        )
        tile_terms = jnp.stack(
            [
                key_grad.reshape(8, BLOCK_TOKENS, kv_width),
                value_grad.reshape(8, BLOCK_TOKENS, kv_width),
            ],
            axis=1,
        )
        return (
            unused_state,
            (
                out_low.reshape(BLOCK_TOKENS, heads_q, head_width),
                query_grad.astype(jnp.bfloat16).reshape(BLOCK_TOKENS, heads_q, head_width),
                tile_terms,
            ),
        )

    unused_final, (output_block_rows, query_gradient_rows, tile_grads) = lax.scan(
        attend,
        0,
        (
            query_loc.reshape(blocks, BLOCK_TOKENS, heads_q, head_width),
            grad_loc.reshape(blocks, BLOCK_TOKENS, heads_q, head_width),
            random_by_block,
            live,
            jnp.arange(blocks),
        ),
    )
    pad_spec_low = ((0, 2), (0, 0), (0, 0), (0, 0))
    pad_spec_mid = ((1, 1), (0, 0), (0, 0), (0, 0))
    pad_spec_high = ((2, 0), (0, 0), (0, 0), (0, 0))
    window_sum = (
        jnp.pad(tile_grads[:, 0], pad_spec_low)
        + jnp.pad(tile_grads[:, 1], pad_spec_mid)
        + jnp.pad(tile_grads[:, 2], pad_spec_high)
    )
    rims = jnp.concatenate([window_sum[0], window_sum[blocks + 1]], axis=1)
    returned_rims = padded(rims.astype(jnp.bfloat16), (("seq", 1),), BLOCK_TOKENS).astype(
        rims.dtype
    )
    interior = window_sum[1 : blocks + 1]
    interior = (
        interior.at[0]
        .add(returned_rims[:, :BLOCK_TOKENS])
        .at[blocks - 1]
        .add(returned_rims[:, 3 * BLOCK_TOKENS :])
    )
    global_terms = jnp.sum(tile_grads[:, 3:5], axis=0)
    global_total = tree_sum(global_terms, "seq")
    own_weight = own_global.astype(jnp.float32)[:, :, None, None, None]
    interior = interior + jnp.sum(own_weight * global_total[:, None], axis=0)
    random_terms = (
        tile_grads[:, 5:8]
        .transpose(1, 0, 2, 3, 4)
        .reshape(entry_count, 2, BLOCK_TOKENS, kv_width)
        .astype(jnp.bfloat16)
    )
    slot_onehot = (my_slot[:, None] == jnp.arange(seq_count * capacity)[None, :]).astype(
        jnp.bfloat16
    )
    back_buffer = jnp.einsum(
        "es,exbw->sxbw", slot_onehot, random_terms, preferred_element_type=jnp.float32
    ).astype(jnp.bfloat16)
    returned_terms = lax.all_to_all(back_buffer, "seq", split_axis=0, concat_axis=0, tiled=True)
    interior = interior + jnp.einsum(
        "tco,tcxbw->oxbw",
        selector,
        returned_terms.reshape(seq_count, capacity, 2, BLOCK_TOKENS, kv_width),
        preferred_element_type=jnp.float32,
    )
    kv_grad = interior.transpose(1, 0, 2, 3).reshape(2, shard_len, kv_width).astype(jnp.bfloat16)
    out_all = output_block_rows.reshape(shard_len, heads_q, head_width)
    query_grad_all = query_gradient_rows.reshape(shard_len, heads_q, head_width)
    key_grad_all = kv_grad[0].reshape(shard_len, heads_kv, head_width)
    value_grad_all = kv_grad[1].reshape(shard_len, heads_kv, head_width)
    return ((out_all, query_grad_all, key_grad_all, value_grad_all), gate)


def head_part(array, chunks, chunk):
    tokens, heads, width = array.shape
    lanes = chunks * lax.axis_size("head")
    grid = array.reshape(tokens, lanes // chunks, chunks, heads // lanes, width)
    return grid[:, :, chunk].reshape(tokens, heads // chunks, width)


def head_join(parts):
    tokens, heads, width = parts[0].shape
    lanes = lax.axis_size("head")
    grid = jnp.stack([p.reshape(tokens, lanes, heads // lanes, width) for p in parts], axis=2)
    return grid.reshape(tokens, heads * len(parts), width)


def per_device(queries, keys, values, output_gradient, global_blocks, random_blocks):
    chunks = max(1, keys.shape[1] // lax.axis_size("head"))
    results = []
    gate = None
    for chunk in range(chunks):
        local, passed = per_chunk(
            head_part(queries, chunks, chunk),
            head_part(keys, chunks, chunk),
            head_part(values, chunks, chunk),
            head_part(output_gradient, chunks, chunk),
            global_blocks,
            random_blocks,
            gate,
        )
        if passed is not None:
            results.append(tuple((head_exchange(x, 0, 1) for x in passed)))
        gate = local
    results.append(tuple((head_exchange(x, 0, 1) for x in gate)))
    return tuple((head_join([r[i] for r in results]) for i in range(4)))


def solution(mesh):
    placed = (
        P(("seq", "head"), None, None),
        P(("seq", "head"), None, None),
        P(("seq", "head"), None, None),
        P(("seq", "head"), None, None),
        P(),
        P(),
    )
    return jax.shard_map(
        per_device,
        mesh=mesh,
        in_specs=placed,
        out_specs=(
            P(("seq", "head"), None, None),
            P(("seq", "head"), None, None),
            P(("seq", "head"), None, None),
            P(("seq", "head"), None, None),
        ),
        check_vma=False,
    )
```

profile of v0, /device:TPU:0, one launch (start us, length us, event | category | flops | bytes accessed | tf_op | source)
XLA Modules:
  0.0 592.3 jit_solution(5233339170795102321)
XLA Ops:
  9.5 6.3 %all-to-all-start.2 = ((bf16[128,4,128]{2,0,1:T(8,128)(2,1)}), bf16[128,4,128]{2,0,1:T(8,128)(2,1)S(1)}, u32[]{:S(2)}, u32[]{:S(2)}) async-start(bf16[128,4,128]{2,0,1:T(8,128)(2,1)} %bitcast.637), calls=%async_computation.2 | async-start | bytes 262144 | tf_op jit(solution)/shard_map/all_to_all | solution.py:65
  17.4 4.5 all-to-all-done.2
  21.9 8.4 %all_to_all.136 = bf16[128,4,128]{2,0,1:T(8,128)(2,1)S(1)} all-to-all(bf16[128,4,128]{2,0,1:T(8,128)(2,1)S(1)} %bitcast.819), channel_id=1, replica_groups=mesh['seq'=8,'head'=4] {'head'}, dimensions={1} | all-to-all | bytes 262144 | tf_op jit(solution)/shard_map/all_to_all | solution.py:66
  31.8 3.3 all-to-all-start.7
  35.8 5.2 all-to-all-done.7
  41.0 4.0 all-to-all-start.8
  46.7 4.2 all-to-all-done.8
  50.9 4.2 all-to-all-start.4
  56.9 20.2 %all-to-all-done.4 = bf16[128,32,128]{2,0,1:T(8,128)(2,1)} async-done(((bf16[128,32,128]{2,0,1:T(8,128)(2,1)}), bf16[128,32,128]{2,0,1:T(8,128)(2,1)}, u32[]{:S(2)}, u32[]{:S(2)}) %all-to-all-start.4) | async-done | bytes 1048608 | tf_op jit(solution)/shard_map/all_to_all | solution.py:64
  77.1 3.5 all-to-all-start
  90.6 13.8 %all-to-all-done = bf16[128,32,128]{2,0,1:T(8,128)(2,1)S(1)} async-done(((bf16[128,32,128]{2,0,1:T(8,128)(2,1)}), bf16[128,32,128]{2,0,1:T(8,128)(2,1)S(1)}, u32[]{:S(2)}, u32[]{:S(2)}) %all-to-all-start) | async-done | bytes 1048608 | tf_op jit(solution)/shard_map/all_to_all | solution.py:64
  104.4 3.5 all-to-all-start.1
  116.1 17.1 %all-to-all-done.1 = bf16[128,32,128]{2,0,1:T(8,128)(2,1)S(1)} async-done(((bf16[128,32,128]{2,0,1:T(8,128)(2,1)}), bf16[128,32,128]{2,0,1:T(8,128)(2,1)S(1)}, u32[]{:S(2)}, u32[]{:S(2)}) %all-to-all-start.1) | async-done | bytes 1048608 | tf_op jit(solution)/shard_map/all_to_all | solution.py:67
  133.2 4.3 all-to-all-start.5
  142.0 4.6 collective-permute-start.10
  172.1 89.8 %while.32 = (s32[]{:T(128)}, bf16[4,128,8,128]{3,2,1,0:T(8,128)(2,1)}, bf16[4,128,8,128]{3,2,1,0:T(8,128)(2,1)}, f32[4,8,2,128,128]{3,4,1,2,0:T(8,128)}, s32[4]{...) while((s32[]{:T(128)}, ...), condition=%wide.region_5.8_spmd, body=%wide.region_1.7_spmd.sunk | while | flops 1632367616 | bytes 61382416 | solution.py:200
  179.7 2.8 copy.654
  186.3 3.6 fusion.183
  208.8 3.5 fusion.183
  224.6 2.8 copy.654
  231.2 3.6 fusion.183
  253.6 3.6 fusion.183
  263.1 5.4 copy.496
  271.6 3.0 collective-permute-start.4
  278.2 6.1 %collective-permute-start.5 = (bf16[2,2,128,128]{2,3,0,1:T(8,128)(2,1)S(1)}, bf16[2,2,128,128]{2,3,0,1:T(8,128)(2,1)S(1)}, u32[]{:S(2)}, u32[]{:S(2)}) collective-permute-start(bf16[2,2,128,128]{2,3,0,1:T(8,128)(2,1)S(1)} %fusion.89), channel_id=1, source_target_pairs={{0,8},{4,12},{8,0},{12,4},{16,24},{20,28},{24,16},{28,20},{1,9},{5... | collective-permute-start | bytes 393224 | tf_op jit(solution)/shard_map/ppermute | solution.py:35
  286.2 3.7 all-to-all-start.6
  292.6 3.1 scatter-add.15
  295.7 11.4 %collective-permute-done.6 = bf16[2,2,128,128]{2,3,0,1:T(8,128)(2,1)S(1)} collective-permute-done((bf16[2,2,128,128]{2,3,0,1:T(8,128)(2,1)S(1)}, bf16[2,2,128,128]{2,3,0,1:T(8,128)(2,1)S(1)}, u32[]{:S(2)}, u32[]{:S(2)}) %collective-permute-start.6) | collective-permute-done | bytes 131104 | tf_op jit(solution)/shard_map/ppermute | solution.py:35
  314.7 109.1 %while.33 = (s32[]{:T(128)}, bf16[4,128,8,128]{3,2,1,0:T(8,128)(2,1)}, bf16[4,128,8,128]{3,2,1,0:T(8,128)(2,1)}, f32[4,8,2,128,128]{3,4,1,2,0:T(8,128)}, s32[4]{...) while((s32[]{:T(128)}, ...), condition=%wide.region_13.17_spmd, body=%wide.region_9.16_spmd.sunk | while | flops 1632367616 | bytes 79207432 | solution.py:200
  326.6 3.6 fusion.196
  353.9 3.6 fusion.196
  381.1 3.6 fusion.196
  408.4 3.6 fusion.196
  425.2 5.4 copy.529
  442.1 3.2 collective-permute-start.24
  447.2 4.2 all-to-all-start.9
  470.6 3.1 scatter-add.19
  474.8 2.9 collective-permute-start.20
  478.4 6.5 %collective-permute-done.8 = bf16[128,8,128]{2,1,0:T(8,128)(2,1)} collective-permute-done((bf16[128,8,128]{2,1,0:T(8,128)(2,1)S(1)}, bf16[128,8,128]{2,1,0:T(8,128)(2,1)}, u32[]{:S(2)}, u32[]{:S(2)}) %collective-permute-start.8) | collective-permute-done | bytes 262176 | tf_op jit(solution)/shard_map/ppermute | solution.py:51
  485.0 3.9 collective-permute-start.12
  488.9 14.7 %collective-permute-start.13 = (bf16[128,8,128]{2,1,0:T(8,128)(2,1)}, bf16[128,8,128]{2,1,0:T(8,128)(2,1)}, u32[]{:S(2)}, u32[]{:S(2)}) collective-permute-start(bf16[128,8,128]{2,1,0:T(8,128)(2,1)} %get-tuple-element.456), channel_id=1, source_target_pairs={{0,2},{1,3},{2,0},{3,1},{4,6},{5,7},{6,4},{7,5},{8,10},{9,11},{10,... | collective-permute-start | bytes 786440 | tf_op jit(solution)/shard_map/ppermute | solution.py:51
  506.1 12.5 %collective-permute-done.19 = bf16[128,8,128]{2,1,0:T(8,128)(2,1)S(1)} collective-permute-done((bf16[128,8,128]{2,1,0:T(8,128)(2,1)}, bf16[128,8,128]{2,1,0:T(8,128)(2,1)S(1)}, u32[]{:S(2)}, u32[]{:S(2)}) %collective-permute-start.19) | collective-permute-done | bytes 262176 | tf_op jit(solution)/shard_map/ppermute | solution.py:51
  518.6 4.1 collective-permute-start.15
  528.7 3.3 collective-permute-start.16
  534.5 6.7 %collective-permute-done.13 = bf16[128,8,128]{2,1,0:T(8,128)(2,1)} collective-permute-done((bf16[128,8,128]{2,1,0:T(8,128)(2,1)}, bf16[128,8,128]{2,1,0:T(8,128)(2,1)}, u32[]{:S(2)}, u32[]{:S(2)}) %collective-permute-start.13) | collective-permute-done | bytes 262176 | tf_op jit(solution)/shard_map/ppermute | solution.py:51
  548.0 4.4 collective-permute-done.16
  554.7 2.9 gather_fusion.6
  567.2 6.1 %collective-permute-start.35 = (bf16[128,1,128]{2,0,1:T(8,128)(2,1)S(1)}, bf16[128,1,128]{2,0,1:T(8,128)(2,1)S(1)}, u32[]{:S(2)}, u32[]{:S(2)}) collective-permute-start(bf16[128,1,128]{2,0,1:T(8,128)(2,1)S(1)} %get-tuple-element.481), channel_id=1, source_target_pairs={{0,1},{1,2},{2,3},{3,0},{4,5},{5,6},{6,7},{7,4},{8,9},{9,10},{10,1... | collective-permute-start | bytes 98312 | tf_op jit(solution)/shard_map/ppermute | solution.py:51
  (482 shorter events, 312.9 us)
Async XLA Ops:
  9.5 12.4 %all-to-all-start.2 = ((bf16[128,4,128]{2,0,1:T(8,128)(2,1)}), bf16[128,4,128]{2,0,1:T(8,128)(2,1)S(1)}, u32[]{:S(2)}, u32[]{:S(2)}) async-start(bf16[128,4,128]{2,0,1:T(8,128)(2,1)} %bitcast.637), calls=%async_computation.2 | async-start | bytes 262144 | tf_op jit(solution)/shard_map/all_to_all | solution.py:65
  15.8 140.3 %all-gather.3.cloned.1.call-start = ((), (), s32[]{:S(2)}) async-start(), calls=%async_computation.10 | async-start | bytes 2359296 | tf_op jit(solution)/shard_map/all_gather | solution.py:117
  31.8 9.2 %all-to-all-start.7 = ((bf16[128,4,128]{2,0,1:T(8,128)(2,1)}), bf16[128,4,128]{2,0,1:T(8,128)(2,1)S(1)}, u32[]{:S(2)}, u32[]{:S(2)}) async-start(bf16[128,4,128]{2,0,1:T(8,128)(2,1)} %bitcast.635), calls=%async_computation.7 | async-start | bytes 262144 | tf_op jit(solution)/shard_map/all_to_all | solution.py:65
  41.0 9.9 %all-to-all-start.8 = ((bf16[128,4,128]{2,0,1:T(8,128)(2,1)}), bf16[128,4,128]{2,0,1:T(8,128)(2,1)}, u32[]{:S(2)}, u32[]{:S(2)}) async-start(bf16[128,4,128]{2,0,1:T(8,128)(2,1)} %bitcast.634), calls=%async_computation.8 | async-start | bytes 262144 | tf_op jit(solution)/shard_map/all_to_all | solution.py:66
  50.9 26.2 %all-to-all-start.4 = ((bf16[128,32,128]{2,0,1:T(8,128)(2,1)}), bf16[128,32,128]{2,0,1:T(8,128)(2,1)}, u32[]{:S(2)}, u32[]{:S(2)}) async-start(bf16[128,32,128]{2,0,1:T(8,128)(2,1)} %bitcast.135), calls=%async_computation.4 | async-start | bytes 2097152 | tf_op jit(solution)/shard_map/all_to_all | solution.py:64
  77.1 27.3 %all-to-all-start = ((bf16[128,32,128]{2,0,1:T(8,128)(2,1)}), bf16[128,32,128]{2,0,1:T(8,128)(2,1)S(1)}, u32[]{:S(2)}, u32[]{:S(2)}) async-start(bf16[128,32,128]{2,0,1:T(8,128)(2,1)} %bitcast.105), calls=%async_computation | async-start | bytes 2097152 | tf_op jit(solution)/shard_map/all_to_all | solution.py:64
  80.6 77.8 %all-gather.5.cloned.1.call-start = ((), (), s32[]{:S(2)}) async-start(), calls=%async_computation.11 | async-start | bytes 2359296 | tf_op jit(solution)/shard_map/all_gather | solution.py:117
  104.4 28.8 %all-to-all-start.1 = ((bf16[128,32,128]{2,0,1:T(8,128)(2,1)}), bf16[128,32,128]{2,0,1:T(8,128)(2,1)S(1)}, u32[]{:S(2)}, u32[]{:S(2)}) async-start(bf16[128,32,128]{2,0,1:T(8,128)(2,1)} %bitcast.111), calls=%async_computation.1 | async-start | bytes 2097152 | tf_op jit(solution)/shard_map/all_to_all | solution.py:67
  133.2 34.1 %all-to-all-start.5 = ((bf16[128,32,128]{0,2,1:T(8,128)(2,1)}), bf16[128,32,128]{0,2,1:T(8,128)(2,1)}, u32[]{:S(2)}, u32[]{:S(2)}) async-start(bf16[128,32,128]{0,2,1:T(8,128)(2,1)} %bitcast.138), calls=%async_computation.5 | async-start | bytes 2097152 | tf_op jit(solution)/shard_map/all_to_all | solution.py:67
  138.6 9.8 %collective-permute-start = (bf16[2,128,128]{2,1,0:T(8,128)(2,1)S(1)}, bf16[2,128,128]{2,1,0:T(8,128)(2,1)S(1)}, u32[]{:S(2)}, u32[]{:S(2)}) collective-permute-start(bf16[2,128,128]{2,1,0:T(8,128)(2,1)S(1)} %get-tuple-element.466), channel_id=1, source_target_pairs={{0,4},{4,8},{8,12},{12,16},{16,20},{20,24},{24,28},{1,5},{5,9},{9,... | collective-permute-start | bytes 196616 | tf_op jit(solution)/shard_map/ppermute | solution.py:17
  139.9 8.5 %collective-permute-start.1 = (bf16[2,128,128]{2,1,0:T(8,128)(2,1)S(1)}, bf16[2,128,128]{2,1,0:T(8,128)(2,1)S(1)}, u32[]{:S(2)}, u32[]{:S(2)}) collective-permute-start(bf16[2,128,128]{2,1,0:T(8,128)(2,1)S(1)} %get-tuple-element.467), channel_id=1, source_target_pairs={{4,0},{8,4},{12,8},{16,12},{20,16},{24,20},{28,24},{5,1},{9,5},{13... | collective-permute-start | bytes 196616 | tf_op jit(solution)/shard_map/ppermute | solution.py:18
  142.0 6.4 %collective-permute-start.10 = (bf16[2,128,128]{2,1,0:T(8,128)(2,1)S(1)}, bf16[2,128,128]{2,1,0:T(8,128)(2,1)S(1)}, u32[]{:S(2)}, u32[]{:S(2)}) collective-permute-start(bf16[2,128,128]{2,1,0:T(8,128)(2,1)S(1)} %get-tuple-element.472), channel_id=1, source_target_pairs={{0,4},{4,8},{8,12},{12,16},{16,20},{20,24},{24,28},{1,5},{5,9},{9,... | collective-permute-start | bytes 196616 | tf_op jit(solution)/shard_map/ppermute | solution.py:17
  146.6 4.4 collective-permute-start.11
  271.6 6.5 %collective-permute-start.4 = (bf16[2,2,128,128]{2,3,0,1:T(8,128)(2,1)S(1)}, bf16[2,2,128,128]{2,3,0,1:T(8,128)(2,1)S(1)}, u32[]{:S(2)}, u32[]{:S(2)}) collective-permute-start(bf16[2,2,128,128]{2,3,0,1:T(8,128)(2,1)S(1)} %convert_element_type.193), channel_id=1, source_target_pairs={{0,4},{4,0},{8,12},{12,8},{16,20},{20,16},{24,28},{28,24},{1,5},{5... | collective-permute-start | bytes 393224 | tf_op jit(solution)/shard_map/ppermute | solution.py:35
  274.8 17.3 %collective-permute-start.2 = (bf16[2,128,128]{2,1,0:T(8,128)(2,1)S(1)}, bf16[2,128,128]{2,1,0:T(8,128)(2,1)S(1)}, u32[]{:S(2)}, u32[]{:S(2)}) collective-permute-start(bf16[2,128,128]{2,1,0:T(8,128)(2,1)S(1)} %get-tuple-element.460), channel_id=1, source_target_pairs={{0,4},{4,8},{8,12},{12,16},{16,20},{20,24},{24,28},{1,5},{5,9},{9,... | collective-permute-start | bytes 196616 | tf_op jit(solution)/shard_map/ppermute | solution.py:17
  276.8 15.2 %collective-permute-start.3 = (bf16[2,128,128]{2,1,0:T(8,128)(2,1)S(1)}, bf16[2,128,128]{2,1,0:T(8,128)(2,1)S(1)}, u32[]{:S(2)}, u32[]{:S(2)}) collective-permute-start(bf16[2,128,128]{2,1,0:T(8,128)(2,1)S(1)} %get-tuple-element.461), channel_id=1, source_target_pairs={{4,0},{8,4},{12,8},{16,12},{20,16},{24,20},{28,24},{5,1},{9,5},{13... | collective-permute-start | bytes 196616 | tf_op jit(solution)/shard_map/ppermute | solution.py:18
  278.2 11.8 %collective-permute-start.5 = (bf16[2,2,128,128]{2,3,0,1:T(8,128)(2,1)S(1)}, bf16[2,2,128,128]{2,3,0,1:T(8,128)(2,1)S(1)}, u32[]{:S(2)}, u32[]{:S(2)}) collective-permute-start(bf16[2,2,128,128]{2,3,0,1:T(8,128)(2,1)S(1)} %fusion.89), channel_id=1, source_target_pairs={{0,8},{4,12},{8,0},{12,4},{16,24},{20,28},{24,16},{28,20},{1,9},{5... | collective-permute-start | bytes 393224 | tf_op jit(solution)/shard_map/ppermute | solution.py:35
  286.2 21.3 %all-to-all-start.6 = ((bf16[16,2,128,128]{3,2,1,0:T(8,128)(2,1)}), bf16[16,2,128,128]{3,2,1,0:T(8,128)(2,1)S(1)}, u32[]{:S(2)}, u32[]{:S(2)}) async-start(bf16[16,2,128,128]{3,2,1,0:T(8,128)(2,1)} %copy.513), calls=%async_computation.6 | async-start | bytes 2097152 | tf_op jit(solution)/shard_map/all_to_all | solution.py:246
  290.0 17.1 %collective-permute-start.6 = (bf16[2,2,128,128]{2,3,0,1:T(8,128)(2,1)S(1)}, bf16[2,2,128,128]{2,3,0,1:T(8,128)(2,1)S(1)}, u32[]{:S(2)}, u32[]{:S(2)}) collective-permute-start(bf16[2,2,128,128]{2,3,0,1:T(8,128)(2,1)S(1)} %fusion.99), channel_id=1, source_target_pairs={{0,16},{4,20},{8,24},{12,28},{16,0},{20,4},{24,8},{28,12},{1,17},{... | collective-permute-start | bytes 393224 | tf_op jit(solution)/shard_map/ppermute | solution.py:35
  434.3 21.3 %collective-permute-start.21 = (bf16[128,1,128]{2,0,1:T(8,128)(2,1)}, bf16[128,1,128]{2,0,1:T(8,128)(2,1)}, u32[]{:S(2)}, u32[]{:S(2)}) collective-permute-start(bf16[128,1,128]{2,0,1:T(8,128)(2,1)} %get-tuple-element.485), channel_id=1, source_target_pairs={{0,1},{1,2},{2,3},{3,0},{4,5},{5,6},{6,7},{7,4},{8,9},{9,10},{10,1... | collective-permute-start | bytes 98312 | tf_op jit(solution)/shard_map/ppermute | solution.py:51
  436.3 19.9 %collective-permute-start.22 = (bf16[128,1,128]{2,0,1:T(8,128)(2,1)}, bf16[128,1,128]{2,0,1:T(8,128)(2,1)}, u32[]{:S(2)}, u32[]{:S(2)}) collective-permute-start(bf16[128,1,128]{2,0,1:T(8,128)(2,1)} %get-tuple-element.484), channel_id=1, source_target_pairs={{0,2},{1,3},{2,0},{3,1},{4,6},{5,7},{6,4},{7,5},{8,10},{9,11},{10,... | collective-permute-start | bytes 98312 | tf_op jit(solution)/shard_map/ppermute | solution.py:51
  438.2 18.9 %collective-permute-start.23 = (bf16[128,1,128]{2,0,1:T(8,128)(2,1)}, bf16[128,1,128]{2,0,1:T(8,128)(2,1)}, u32[]{:S(2)}, u32[]{:S(2)}) collective-permute-start(bf16[128,1,128]{2,0,1:T(8,128)(2,1)} %get-tuple-element.483), channel_id=1, source_target_pairs={{0,3},{1,0},{2,1},{3,2},{4,7},{5,4},{6,5},{7,6},{8,11},{9,8},{10,9... | collective-permute-start | bytes 98312 | tf_op jit(solution)/shard_map/ppermute | solution.py:51
  440.4 33.2 %collective-permute-start.26 = (bf16[2,2,128,128]{2,3,0,1:T(8,128)(2,1)}, bf16[2,2,128,128]{2,3,0,1:T(8,128)(2,1)S(1)}, u32[]{:S(2)}, u32[]{:S(2)}) collective-permute-start(bf16[2,2,128,128]{2,3,0,1:T(8,128)(2,1)} %convert_element_type.207), channel_id=1, source_target_pairs={{0,4},{4,0},{8,12},{12,8},{16,20},{20,16},{24,28},{28,24},{1,5},{5... | collective-permute-start | bytes 393224 | tf_op jit(solution)/shard_map/ppermute | solution.py:35
  442.1 24.4 %collective-permute-start.24 = (bf16[2,128,128]{2,1,0:T(8,128)(2,1)}, bf16[2,128,128]{2,1,0:T(8,128)(2,1)}, u32[]{:S(2)}, u32[]{:S(2)}) collective-permute-start(bf16[2,128,128]{2,1,0:T(8,128)(2,1)} %get-tuple-element.458), channel_id=1, source_target_pairs={{0,4},{4,8},{8,12},{12,16},{16,20},{20,24},{24,28},{1,5},{5,9},{9,... | collective-permute-start | bytes 196616 | tf_op jit(solution)/shard_map/ppermute | solution.py:17
  447.2 117.6 %all-to-all-start.9 = ((bf16[16,2,128,128]{3,2,1,0:T(8,128)(2,1)}), bf16[16,2,128,128]{3,2,1,0:T(8,128)(2,1)}, u32[]{:S(2)}, u32[]{:S(2)}) async-start(bf16[16,2,128,128]{3,2,1,0:T(8,128)(2,1)} %copy.538), calls=%async_computation.9 | async-start | bytes 2097152 | tf_op jit(solution)/shard_map/all_to_all | solution.py:246
  455.6 6.1 %collective-permute-start.32 = (bf16[128,1,128]{2,0,1:T(8,128)(2,1)S(1)}, bf16[128,1,128]{2,0,1:T(8,128)(2,1)S(1)}, u32[]{:S(2)}, u32[]{:S(2)}) collective-permute-start(bf16[128,1,128]{2,0,1:T(8,128)(2,1)S(1)} %get-tuple-element.477), channel_id=1, source_target_pairs={{0,1},{1,2},{2,3},{3,0},{4,5},{5,6},{6,7},{7,4},{8,9},{9,10},{10,1... | collective-permute-start | bytes 98312 | tf_op jit(solution)/shard_map/ppermute | solution.py:51
  456.2 6.8 %collective-permute-start.33 = (bf16[128,1,128]{2,0,1:T(8,128)(2,1)S(1)}, bf16[128,1,128]{2,0,1:T(8,128)(2,1)S(1)}, u32[]{:S(2)}, u32[]{:S(2)}) collective-permute-start(bf16[128,1,128]{2,0,1:T(8,128)(2,1)S(1)} %get-tuple-element.476), channel_id=1, source_target_pairs={{0,2},{1,3},{2,0},{3,1},{4,6},{5,7},{6,4},{7,5},{8,10},{9,11},{10,... | collective-permute-start | bytes 98312 | tf_op jit(solution)/shard_map/ppermute | solution.py:51
  457.2 6.3 %collective-permute-start.34 = (bf16[128,1,128]{2,0,1:T(8,128)(2,1)S(1)}, bf16[128,1,128]{2,0,1:T(8,128)(2,1)S(1)}, u32[]{:S(2)}, u32[]{:S(2)}) collective-permute-start(bf16[128,1,128]{2,0,1:T(8,128)(2,1)S(1)} %get-tuple-element.475), channel_id=1, source_target_pairs={{0,3},{1,0},{2,1},{3,2},{4,7},{5,4},{6,5},{7,6},{8,11},{9,8},{10,9... | collective-permute-start | bytes 98312 | tf_op jit(solution)/shard_map/ppermute | solution.py:51
  461.7 7.4 %collective-permute-start.25 = (bf16[2,128,128]{2,1,0:T(8,128)(2,1)S(1)}, bf16[2,128,128]{2,1,0:T(8,128)(2,1)S(1)}, u32[]{:S(2)}, u32[]{:S(2)}) collective-permute-start(bf16[2,128,128]{2,1,0:T(8,128)(2,1)S(1)} %copy-done.14), channel_id=1, source_target_pairs={{4,0},{8,4},{12,8},{16,12},{20,16},{24,20},{28,24},{5,1},{9,5},{13... | collective-permute-start | bytes 196616 | tf_op jit(solution)/shard_map/ppermute | solution.py:18
  463.0 11.8 %collective-permute-start.7 = (bf16[128,8,128]{2,1,0:T(8,128)(2,1)S(1)}, bf16[128,8,128]{2,1,0:T(8,128)(2,1)S(1)}, u32[]{:S(2)}, u32[]{:S(2)}) collective-permute-start(bf16[128,8,128]{2,1,0:T(8,128)(2,1)S(1)} %copy-done.22), channel_id=1, source_target_pairs={{0,1},{1,2},{2,3},{3,0},{4,5},{5,6},{6,7},{7,4},{8,9},{9,10},{10,1... | collective-permute-start | bytes 786440 | tf_op jit(solution)/shard_map/ppermute | solution.py:51
  463.5 21.5 %collective-permute-start.8 = (bf16[128,8,128]{2,1,0:T(8,128)(2,1)S(1)}, bf16[128,8,128]{2,1,0:T(8,128)(2,1)}, u32[]{:S(2)}, u32[]{:S(2)}) collective-permute-start(bf16[128,8,128]{2,1,0:T(8,128)(2,1)S(1)} %copy-done.21), channel_id=1, source_target_pairs={{0,2},{1,3},{2,0},{3,1},{4,6},{5,7},{6,4},{7,5},{8,10},{9,11},{10,... | collective-permute-start | bytes 786440 | tf_op jit(solution)/shard_map/ppermute | solution.py:51
  466.5 22.4 %collective-permute-start.9 = (bf16[128,8,128]{2,1,0:T(8,128)(2,1)S(1)}, bf16[128,8,128]{2,1,0:T(8,128)(2,1)}, u32[]{:S(2)}, u32[]{:S(2)}) collective-permute-start(bf16[128,8,128]{2,1,0:T(8,128)(2,1)S(1)} %copy-done.20), channel_id=1, source_target_pairs={{0,3},{1,0},{2,1},{3,2},{4,7},{5,4},{6,5},{7,6},{8,11},{9,8},{10,9... | collective-permute-start | bytes 786440 | tf_op jit(solution)/shard_map/ppermute | solution.py:51
  469.1 35.7 %collective-permute-start.18 = (bf16[128,8,128]{2,1,0:T(8,128)(2,1)}, bf16[128,8,128]{2,1,0:T(8,128)(2,1)}, u32[]{:S(2)}, u32[]{:S(2)}) collective-permute-start(bf16[128,8,128]{2,1,0:T(8,128)(2,1)} %get-tuple-element.449), channel_id=1, source_target_pairs={{0,1},{1,2},{2,3},{3,0},{4,5},{5,6},{6,7},{7,4},{8,9},{9,10},{10,1... | collective-permute-start | bytes 786440 | tf_op jit(solution)/shard_map/ppermute | solution.py:51
  473.7 44.9 %collective-permute-start.19 = (bf16[128,8,128]{2,1,0:T(8,128)(2,1)}, bf16[128,8,128]{2,1,0:T(8,128)(2,1)S(1)}, u32[]{:S(2)}, u32[]{:S(2)}) collective-permute-start(bf16[128,8,128]{2,1,0:T(8,128)(2,1)} %get-tuple-element.448), channel_id=1, source_target_pairs={{0,2},{1,3},{2,0},{3,1},{4,6},{5,7},{6,4},{7,5},{8,10},{9,11},{10,... | collective-permute-start | bytes 786440 | tf_op jit(solution)/shard_map/ppermute | solution.py:51
  474.8 47.9 %collective-permute-start.20 = (bf16[128,8,128]{2,1,0:T(8,128)(2,1)S(1)}, bf16[128,8,128]{2,1,0:T(8,128)(2,1)S(1)}, u32[]{:S(2)}, u32[]{:S(2)}) collective-permute-start(bf16[128,8,128]{2,1,0:T(8,128)(2,1)S(1)} %get-tuple-element.447), channel_id=1, source_target_pairs={{0,3},{1,0},{2,1},{3,2},{4,7},{5,4},{6,5},{7,6},{8,11},{9,8},{10,9... | collective-permute-start | bytes 786440 | tf_op jit(solution)/shard_map/ppermute | solution.py:51
  485.0 47.0 %collective-permute-start.12 = (bf16[128,8,128]{2,1,0:T(8,128)(2,1)}, bf16[128,8,128]{2,1,0:T(8,128)(2,1)}, u32[]{:S(2)}, u32[]{:S(2)}) collective-permute-start(bf16[128,8,128]{2,1,0:T(8,128)(2,1)} %get-tuple-element.457), channel_id=1, source_target_pairs={{0,1},{1,2},{2,3},{3,0},{4,5},{5,6},{6,7},{7,4},{8,9},{9,10},{10,1... | collective-permute-start | bytes 786440 | tf_op jit(solution)/shard_map/ppermute | solution.py:51
  488.9 52.3 %collective-permute-start.13 = (bf16[128,8,128]{2,1,0:T(8,128)(2,1)}, bf16[128,8,128]{2,1,0:T(8,128)(2,1)}, u32[]{:S(2)}, u32[]{:S(2)}) collective-permute-start(bf16[128,8,128]{2,1,0:T(8,128)(2,1)} %get-tuple-element.456), channel_id=1, source_target_pairs={{0,2},{1,3},{2,0},{3,1},{4,6},{5,7},{6,4},{7,5},{8,10},{9,11},{10,... | collective-permute-start | bytes 786440 | tf_op jit(solution)/shard_map/ppermute | solution.py:51
  504.9 38.8 %collective-permute-start.14 = (bf16[128,8,128]{2,1,0:T(8,128)(2,1)}, bf16[128,8,128]{2,1,0:T(8,128)(2,1)}, u32[]{:S(2)}, u32[]{:S(2)}) collective-permute-start(bf16[128,8,128]{2,1,0:T(8,128)(2,1)} %get-tuple-element.455), channel_id=1, source_target_pairs={{0,3},{1,0},{2,1},{3,2},{4,7},{5,4},{6,5},{7,6},{8,11},{9,8},{10,9... | collective-permute-start | bytes 786440 | tf_op jit(solution)/shard_map/ppermute | solution.py:51
  518.6 29.4 %collective-permute-start.15 = (bf16[128,8,128]{2,1,0:T(8,128)(2,1)}, bf16[128,8,128]{2,1,0:T(8,128)(2,1)}, u32[]{:S(2)}, u32[]{:S(2)}) collective-permute-start(bf16[128,8,128]{2,1,0:T(8,128)(2,1)} %get-tuple-element.445), channel_id=1, source_target_pairs={{0,1},{1,2},{2,3},{3,0},{4,5},{5,6},{6,7},{7,4},{8,9},{9,10},{10,1... | collective-permute-start | bytes 786440 | tf_op jit(solution)/shard_map/ppermute | solution.py:51
  522.7 6.0 %collective-permute-start.27 = (bf16[2,2,128,128]{2,3,0,1:T(8,128)(2,1)}, bf16[2,2,128,128]{2,3,0,1:T(8,128)(2,1)}, u32[]{:S(2)}, u32[]{:S(2)}) collective-permute-start(bf16[2,2,128,128]{2,3,0,1:T(8,128)(2,1)} %fusion.90), channel_id=1, source_target_pairs={{0,8},{4,12},{8,0},{12,4},{16,24},{20,28},{24,16},{28,20},{1,9},{5... | collective-permute-start | bytes 393224 | tf_op jit(solution)/shard_map/ppermute | solution.py:35
  528.7 23.7 %collective-permute-start.16 = (bf16[128,8,128]{2,1,0:T(8,128)(2,1)}, bf16[128,8,128]{2,1,0:T(8,128)(2,1)}, u32[]{:S(2)}, u32[]{:S(2)}) collective-permute-start(bf16[128,8,128]{2,1,0:T(8,128)(2,1)} %get-tuple-element.444), channel_id=1, source_target_pairs={{0,2},{1,3},{2,0},{3,1},{4,6},{5,7},{6,4},{7,5},{8,10},{9,11},{10,... | collective-permute-start | bytes 786440 | tf_op jit(solution)/shard_map/ppermute | solution.py:51
  531.9 20.4 %collective-permute-start.17 = (bf16[128,8,128]{2,1,0:T(8,128)(2,1)}, bf16[128,8,128]{2,1,0:T(8,128)(2,1)}, u32[]{:S(2)}, u32[]{:S(2)}) collective-permute-start(bf16[128,8,128]{2,1,0:T(8,128)(2,1)} %get-tuple-element.443), channel_id=1, source_target_pairs={{0,3},{1,0},{2,1},{3,2},{4,7},{5,4},{6,5},{7,6},{8,11},{9,8},{10,9... | collective-permute-start | bytes 786440 | tf_op jit(solution)/shard_map/ppermute | solution.py:51
  541.2 22.3 %collective-permute-start.28 = (bf16[2,2,128,128]{2,3,0,1:T(8,128)(2,1)}, bf16[2,2,128,128]{2,3,0,1:T(8,128)(2,1)}, u32[]{:S(2)}, u32[]{:S(2)}) collective-permute-start(bf16[2,2,128,128]{2,3,0,1:T(8,128)(2,1)} %fusion.100), channel_id=1, source_target_pairs={{0,16},{4,20},{8,24},{12,28},{16,0},{20,4},{24,8},{28,12},{1,17},{... | collective-permute-start | bytes 393224 | tf_op jit(solution)/shard_map/ppermute | solution.py:35
  567.2 11.2 %collective-permute-start.35 = (bf16[128,1,128]{2,0,1:T(8,128)(2,1)S(1)}, bf16[128,1,128]{2,0,1:T(8,128)(2,1)S(1)}, u32[]{:S(2)}, u32[]{:S(2)}) collective-permute-start(bf16[128,1,128]{2,0,1:T(8,128)(2,1)S(1)} %get-tuple-element.481), channel_id=1, source_target_pairs={{0,1},{1,2},{2,3},{3,0},{4,5},{5,6},{6,7},{7,4},{8,9},{9,10},{10,1... | collective-permute-start | bytes 98312 | tf_op jit(solution)/shard_map/ppermute | solution.py:51
  573.3 6.4 %collective-permute-start.36 = (bf16[128,1,128]{2,0,1:T(8,128)(2,1)S(1)}, bf16[128,1,128]{2,0,1:T(8,128)(2,1)S(1)}, u32[]{:S(2)}, u32[]{:S(2)}) collective-permute-start(bf16[128,1,128]{2,0,1:T(8,128)(2,1)S(1)} %get-tuple-element.480), channel_id=1, source_target_pairs={{0,2},{1,3},{2,0},{3,1},{4,6},{5,7},{6,4},{7,5},{8,10},{9,11},{10,... | collective-permute-start | bytes 98312 | tf_op jit(solution)/shard_map/ppermute | solution.py:51
  574.7 5.0 collective-permute-start.37
  575.8 5.9 collective-permute-start.29
  576.8 5.8 collective-permute-start.30
  (54 other events, 732.7 us)
Sparse Core Ops, SparseCore 0:
  31.2 26.8 all-gather.2
  84.2 29.0 all-gather.4
where the time goes:
time: 601 us; the launch traced here: 592 us
  local copies, waits for them, and re-layouts  168 us (28%)
  starting transfers between devices  129 us (21%)
  waiting for transfers between devices  112 us (19%)
  matrix products  86.2 us (14%)
  other arithmetic  67.2 us (11%)
  between operations  15.3 us (3%)
  blocking collectives  8.43 us (1%)
  loops' own time  6.06 us (1%)
    ppermute x24, starting transfers between devices, head_exchange(): part = lax.ppermute(part, 'head', pairs)  58.8 us
    another operation x20, local copies, waits for them, and re-layouts  35.9 us
    all_to_all x2, waiting for transfers between devices, per_chunk(): lax.all_to_all(queries, 'head', split_axis=1, concat_axis=0, tiled=True)  34 us
    ppermute x24, waiting for transfers between devices, head_exchange(): part = lax.ppermute(part, 'head', pairs)  32.7 us
    dot_general x8, matrix products, attend(): jnp.einsum('qkgd,tbkd->kgqtb', grad_grid, value_t, preferred_element_type...  28.5 us
    dot_general x8, matrix products, attend(): jnp.einsum('kgqtb,qkgd->tbkd', prob_low, grad_grid, preferred_element_typ...  17.2 us
    all_to_all x2, waiting for transfers between devices, per_chunk(): lax.all_to_all(output_gradient, 'head', split_axis=1, concat_axis=0, tile...  17.1 us
    dynamic_slice x24, local copies, waits for them, and re-layouts, per_chunk(): lax.scan(attend, 0, (query_loc.reshape(blocks, BLOCK_TOKENS, heads_q, hea...  16.8 us
  transfers between devices with their start and end apart: 49, of which 16 were waited for; matrix products, arithmetic and copies ran while one was open for 15% of the time, Pallas kernels for 0%

commit v1 on v0

--- a/solution.py
+++ b/solution.py
@@ -60,8 +60,14 @@
 
 
 def per_chunk(queries, keys, values, output_gradient, global_blocks, random_blocks, gate):
+    treat_skins_by_axis = lambda field_in, axis_key: jnp.concatenate(
+        lax.all_to_all(
+            jnp.stack(jnp.split(field_in, lax.axis_size(axis_key), axis=1)), axis_key, 0, 0
+        ),
+        0,
+    )
     query_loc, key_loc, value_loc, grad_loc = (
-        lax.all_to_all(queries, "head", split_axis=1, concat_axis=0, tiled=True),
+        treat_skins_by_axis(queries, axis_key="head"),
         lax.all_to_all(keys, "head", split_axis=1, concat_axis=0, tiled=True),
         lax.all_to_all(values, "head", split_axis=1, concat_axis=0, tiled=True),
         lax.all_to_all(output_gradient, "head", split_axis=1, concat_axis=0, tiled=True),

time: 601 us -> 552 us (0.918)
  waiting for transfers between devices: 112 us -> 54.7 us
  starting transfers between devices: 129 us -> 136 us
    all_to_all x2, waiting for transfers between devices: 34 us -> 13 us  [per_chunk(): lax.all_to_all(jnp.stack(jnp.split(field_in, lax.axis_size(axis_key), axi...]
    all_to_all x2, waiting for transfers between devices: 17.1 us -> 0.46 us  [per_chunk(): lax.all_to_all(output_gradient, 'head', split_axis=1, concat_axis=0, tile...]
    ppermute x6, waiting for transfers between devices: 12 us -> 0.59 us  [tree_sum(): other = lax.ppermute(part.astype(jnp.bfloat16), axis, pairs)]
    ppermute x24, waiting for transfers between devices: 32.7 us -> 26 us  [head_exchange(): part = lax.ppermute(part, 'head', pairs)]
    another operation x20 -> x22, local copies, waits for them, and re-layouts: 35.9 us -> 36.1 us
  transfers between devices with their start and end apart: 49 -> 49, of which waited for: 16 -> 14; matrix products, arithmetic and copies ran while one was open for 15% -> 35% of each run, Pallas kernels for 0% -> 0%
where the time goes in v1:
time: 552 us; the launch traced here: 541 us
  local copies, waits for them, and re-layouts  163 us (30%)
  starting transfers between devices  136 us (25%)
  matrix products  85.5 us (15%)
  other arithmetic  72.8 us (13%)
  waiting for transfers between devices  54.7 us (10%)
  between operations  15.3 us (3%)
  blocking collectives  8.43 us (2%)
  loops' own time  6.28 us (1%)
    ppermute x24, starting transfers between devices, head_exchange(): part = lax.ppermute(part, 'head', pairs)  58.2 us
    another operation x20, local copies, waits for them, and re-layouts  35.8 us
    dot_general x8, matrix products, attend(): jnp.einsum('qkgd,tbkd->kgqtb', grad_grid, value_t, preferred_element_type...  28.4 us
    ppermute x24, waiting for transfers between devices, head_exchange(): part = lax.ppermute(part, 'head', pairs)  26 us
    dot_general x8, matrix products, attend(): jnp.einsum('kgqtb,qkgd->tbkd', prob_low, grad_grid, preferred_element_typ...  17.2 us
    ppermute x6, starting transfers between devices, tree_sum(): other = lax.ppermute(part.astype(jnp.bfloat16), axis, pairs)  17.2 us
    dynamic_slice x24, local copies, waits for them, and re-layouts, per_chunk(): lax.scan(attend, 0, (query_loc.reshape(blocks, BLOCK_TOKENS, heads_q, hea...  16.8 us
    dot_general x8, matrix products, attend(): jnp.einsum('kgqtb,qkgd->tbkd', score_low, query_grid, preferred_element_t...  13.6 us
  transfers between devices with their start and end apart: 49, of which 14 were waited for; matrix products, arithmetic and copies ran while one was open for 35% of the time, Pallas kernels for 0%

profile of v1, /device:TPU:0, one launch (start us, length us, event | category | flops | bytes accessed | tf_op | source)
XLA Modules:
  0.0 541.3 jit_solution(15844338955871956948)
XLA Ops:
  9.4 6.3 %all-to-all-start.2 = ((bf16[128,4,128]{2,0,1:T(8,128)(2,1)}), bf16[128,4,128]{2,0,1:T(8,128)(2,1)S(1)}, u32[]{:S(2)}, u32[]{:S(2)}) async-start(bf16[128,4,128]{2,0,1:T(8,128)(2,1)} %bitcast.648), calls=%async_computation.2 | async-start | bytes 262144 | tf_op jit(solution)/shard_map/all_to_all | solution.py:71
  17.3 4.5 all-to-all-done.2
  21.8 8.4 %all_to_all.113 = bf16[128,4,128]{2,0,1:T(8,128)(2,1)S(1)} all-to-all(bf16[128,4,128]{2,0,1:T(8,128)(2,1)S(1)} %bitcast.833), channel_id=1, replica_groups=mesh['seq'=8,'head'=4] {'head'}, dimensions={1} | all-to-all | bytes 262144 | tf_op jit(solution)/shard_map/all_to_all | solution.py:72
  32.3 3.3 all-to-all-start.7
  41.5 4.9 all-to-all-start.8
  48.1 4.2 all-to-all-done.8
  52.3 4.3 all-to-all-start.4
  73.7 5.2 all-to-all-done.4
  78.9 4.3 all-to-all-start.5
  89.2 5.4 collective-permute-start.10
  107.5 5.1 all-to-all-start.1
  117.4 87.5 %while.32 = (s32[]{:T(128)}, bf16[4,128,8,128]{3,2,1,0:T(8,128)(2,1)}, bf16[4,128,8,128]{3,2,1,0:T(8,128)(2,1)}, f32[4,8,2,128,128]{3,4,1,2,0:T(8,128)}, s32[4]{...) while((s32[]{:T(128)}, ...), condition=%wide.region_5.8_spmd, body=%wide.region_1.7_spmd.sunk | while | flops 1632367616 | bytes 61382912 | solution.py:206
  131.0 3.6 fusion.183
  152.9 3.5 fusion.183
  174.8 3.6 fusion.183
  196.7 3.5 fusion.183
  204.9 5.4 copy.482
  213.8 6.5 %all-to-all-start.6 = ((bf16[16,2,128,128]{3,2,1,0:T(8,128)(2,1)}), bf16[16,2,128,128]{3,2,1,0:T(8,128)(2,1)S(1)}, u32[]{:S(2)}, u32[]{:S(2)}) async-start(bf16[16,2,128,128]{3,2,1,0:T(8,128)(2,1)} %copy.499), calls=%async_computation.6 | async-start | bytes 2097152 | tf_op jit(solution)/shard_map/all_to_all | solution.py:252
  221.9 2.9 copy.471
  230.6 5.5 %all-to-all-done.6 = bf16[16,2,128,128]{3,2,1,0:T(8,128)(2,1)S(1)} async-done(((bf16[16,2,128,128]{3,2,1,0:T(8,128)(2,1)}), bf16[16,2,128,128]{3,2,1,0:T(8,128)(2,1)S(1)}, u32[]{:S(2)}, u32[]{:S(2)}) %all-to-all-start.6) | async-done | bytes 1048608 | tf_op jit(solution)/shard_map/all_to_all | solution.py:252
  236.2 5.1 all-to-all-start
  245.1 4.5 collective-permute-start.6
  250.1 3.1 scatter-add.15
  256.0 7.8 %all-to-all-done = bf16[4,128,8,128]{3,2,1,0:T(8,128)(2,1)} async-done(((bf16[4,128,8,128]{3,2,1,0:T(8,128)(2,1)}), bf16[4,128,8,128]{3,2,1,0:T(8,128)(2,1)}, u32[]{:S(2)}, u32[]{:S(2)}) %all-to-all-start) | async-done | bytes 1048608 | tf_op jit(solution)/shard_map/all_to_all | solution.py:64
  268.5 106.5 %while.33 = (s32[]{:T(128)}, bf16[4,128,8,128]{3,2,1,0:T(8,128)(2,1)}, bf16[4,128,8,128]{3,2,1,0:T(8,128)(2,1)}, f32[4,8,2,128,128]{3,4,1,2,0:T(8,128)}, s32[4]{...) while((s32[]{:T(128)}, ...), condition=%wide.region_13.17_spmd, body=%wide.region_9.16_spmd.sunk | while | flops 1632367616 | bytes 79207600 | solution.py:206
  279.8 3.5 fusion.196
  306.4 3.5 fusion.196
  333.0 3.5 fusion.196
  359.7 3.6 fusion.196
  376.4 5.4 copy.515
  391.7 3.2 collective-permute-start.24
  396.8 4.2 all-to-all-start.9
  407.3 2.8 collective-permute-start.34
  420.7 3.1 scatter-add.19
  425.3 2.9 collective-permute-start.20
  428.9 5.4 %collective-permute-done.8 = bf16[128,8,128]{2,1,0:T(8,128)(2,1)} collective-permute-done((bf16[128,8,128]{2,1,0:T(8,128)(2,1)S(1)}, bf16[128,8,128]{2,1,0:T(8,128)(2,1)}, u32[]{:S(2)}, u32[]{:S(2)}) %collective-permute-start.8) | collective-permute-done | bytes 262176 | tf_op jit(solution)/shard_map/ppermute | solution.py:51
  434.3 3.0 collective-permute-start.12
  437.3 13.3 %collective-permute-start.13 = (bf16[128,8,128]{2,1,0:T(8,128)(2,1)}, bf16[128,8,128]{2,1,0:T(8,128)(2,1)}, u32[]{:S(2)}, u32[]{:S(2)}) collective-permute-start(bf16[128,8,128]{2,1,0:T(8,128)(2,1)} %get-tuple-element.456), channel_id=1, source_target_pairs={{0,2},{1,3},{2,0},{3,1},{4,6},{5,7},{6,4},{7,5},{8,10},{9,11},{10,... | collective-permute-start | bytes 786440 | tf_op jit(solution)/shard_map/ppermute | solution.py:51
  451.8 3.5 collective-permute-start.14
  455.3 12.5 %collective-permute-done.19 = bf16[128,8,128]{2,1,0:T(8,128)(2,1)S(1)} collective-permute-done((bf16[128,8,128]{2,1,0:T(8,128)(2,1)}, bf16[128,8,128]{2,1,0:T(8,128)(2,1)S(1)}, u32[]{:S(2)}, u32[]{:S(2)}) %collective-permute-start.19) | collective-permute-done | bytes 262176 | tf_op jit(solution)/shard_map/ppermute | solution.py:51
  467.9 3.2 collective-permute-start.15
  471.1 5.1 collective-permute-start.27
  479.5 3.3 collective-permute-start.16
  486.0 3.0 collective-permute-done.13
  489.0 5.3 collective-permute-start.28
  498.6 3.1 collective-permute-done.16
  504.0 2.9 gather_fusion.6
  516.5 6.2 %collective-permute-start.35 = (bf16[128,1,128]{2,0,1:T(8,128)(2,1)S(1)}, bf16[128,1,128]{2,0,1:T(8,128)(2,1)S(1)}, u32[]{:S(2)}, u32[]{:S(2)}) collective-permute-start(bf16[128,1,128]{2,0,1:T(8,128)(2,1)S(1)} %get-tuple-element.489), channel_id=1, source_target_pairs={{0,1},{1,2},{2,3},{3,0},{4,5},{5,6},{6,7},{7,4},{8,9},{9,10},{10,1... | collective-permute-start | bytes 98312 | tf_op jit(solution)/shard_map/ppermute | solution.py:51
  (536 shorter events, 303.2 us)
Async XLA Ops:
  9.4 12.4 %all-to-all-start.2 = ((bf16[128,4,128]{2,0,1:T(8,128)(2,1)}), bf16[128,4,128]{2,0,1:T(8,128)(2,1)S(1)}, u32[]{:S(2)}, u32[]{:S(2)}) async-start(bf16[128,4,128]{2,0,1:T(8,128)(2,1)} %bitcast.648), calls=%async_computation.2 | async-start | bytes 262144 | tf_op jit(solution)/shard_map/all_to_all | solution.py:71
  15.7 80.2 %all-gather.3.cloned.1.call-start = ((), (), s32[]{:S(2)}) async-start(), calls=%async_computation.10 | async-start | bytes 2359296 | tf_op jit(solution)/shard_map/all_gather | solution.py:123
  32.3 9.2 %all-to-all-start.7 = ((bf16[128,4,128]{2,0,1:T(8,128)(2,1)}), bf16[128,4,128]{2,0,1:T(8,128)(2,1)S(1)}, u32[]{:S(2)}, u32[]{:S(2)}) async-start(bf16[128,4,128]{2,0,1:T(8,128)(2,1)} %bitcast.646), calls=%async_computation.7 | async-start | bytes 262144 | tf_op jit(solution)/shard_map/all_to_all | solution.py:71
  41.5 10.8 %all-to-all-start.8 = ((bf16[128,4,128]{2,0,1:T(8,128)(2,1)}), bf16[128,4,128]{2,0,1:T(8,128)(2,1)S(1)}, u32[]{:S(2)}, u32[]{:S(2)}) async-start(bf16[128,4,128]{2,0,1:T(8,128)(2,1)} %bitcast.831), calls=%async_computation.8 | async-start | bytes 262144 | tf_op jit(solution)/shard_map/all_to_all | solution.py:72
  52.3 26.6 %all-to-all-start.4 = ((bf16[4,128,8,128]{3,1,2,0:T(8,128)(2,1)}), bf16[4,128,8,128]{3,1,2,0:T(8,128)(2,1)}, u32[]{:S(2)}, u32[]{:S(2)}) async-start(bf16[4,128,8,128]{3,1,2,0:T(8,128)(2,1)} %pad_maximum_fusion.5), calls=%async_computation.4 | async-start | bytes 2097152 | tf_op jit(solution)/shard_map/all_to_all | solution.py:64
  56.6 41.7 %all-gather.5.cloned.1.call-start = ((), (), s32[]{:S(2)}) async-start(), calls=%async_computation.11 | async-start | bytes 2359296 | tf_op jit(solution)/shard_map/all_gather | solution.py:123
  78.9 28.5 %all-to-all-start.5 = ((bf16[128,32,128]{0,2,1:T(8,128)(2,1)}), bf16[128,32,128]{0,2,1:T(8,128)(2,1)}, u32[]{:S(2)}, u32[]{:S(2)}) async-start(bf16[128,32,128]{0,2,1:T(8,128)(2,1)} %bitcast.141), calls=%async_computation.5 | async-start | bytes 2097152 | tf_op jit(solution)/shard_map/all_to_all | solution.py:73
  86.0 9.9 %collective-permute-start = (bf16[2,128,128]{2,1,0:T(8,128)(2,1)S(1)}, bf16[2,128,128]{2,1,0:T(8,128)(2,1)S(1)}, u32[]{:S(2)}, u32[]{:S(2)}) collective-permute-start(bf16[2,128,128]{2,1,0:T(8,128)(2,1)S(1)} %get-tuple-element.474), channel_id=1, source_target_pairs={{0,4},{4,8},{8,12},{12,16},{16,20},{20,24},{24,28},{1,5},{5,9},{9,... | collective-permute-start | bytes 196616 | tf_op jit(solution)/shard_map/ppermute | solution.py:17
  87.3 8.6 %collective-permute-start.1 = (bf16[2,128,128]{2,1,0:T(8,128)(2,1)S(1)}, bf16[2,128,128]{2,1,0:T(8,128)(2,1)S(1)}, u32[]{:S(2)}, u32[]{:S(2)}) collective-permute-start(bf16[2,128,128]{2,1,0:T(8,128)(2,1)S(1)} %get-tuple-element.475), channel_id=1, source_target_pairs={{4,0},{8,4},{12,8},{16,12},{20,16},{24,20},{28,24},{5,1},{9,5},{13... | collective-permute-start | bytes 196616 | tf_op jit(solution)/shard_map/ppermute | solution.py:18
  89.2 131.0 %collective-permute-start.10 = (bf16[2,128,128]{2,1,0:T(8,128)(2,1)}, bf16[2,128,128]{2,1,0:T(8,128)(2,1)}, u32[]{:S(2)}, u32[]{:S(2)}) collective-permute-start(bf16[2,128,128]{2,1,0:T(8,128)(2,1)} %get-tuple-element.480), channel_id=1, source_target_pairs={{0,4},{4,8},{8,12},{12,16},{16,20},{20,24},{24,28},{1,5},{5,9},{9,... | collective-permute-start | bytes 196616 | tf_op jit(solution)/shard_map/ppermute | solution.py:17
  94.6 125.7 %collective-permute-start.11 = (bf16[2,128,128]{2,1,0:T(8,128)(2,1)}, bf16[2,128,128]{2,1,0:T(8,128)(2,1)}, u32[]{:S(2)}, u32[]{:S(2)}) collective-permute-start(bf16[2,128,128]{2,1,0:T(8,128)(2,1)} %get-tuple-element.481), channel_id=1, source_target_pairs={{4,0},{8,4},{12,8},{16,12},{20,16},{24,20},{28,24},{5,1},{9,5},{13... | collective-permute-start | bytes 196616 | tf_op jit(solution)/shard_map/ppermute | solution.py:18
  107.5 106.3 %all-to-all-start.1 = ((bf16[128,32,128]{2,0,1:T(8,128)(2,1)}), bf16[128,32,128]{2,0,1:T(8,128)(2,1)}, u32[]{:S(2)}, u32[]{:S(2)}) async-start(bf16[128,32,128]{2,0,1:T(8,128)(2,1)} %bitcast.112), calls=%async_computation.1 | async-start | bytes 2097152 | tf_op jit(solution)/shard_map/all_to_all | solution.py:73
  213.8 22.4 %all-to-all-start.6 = ((bf16[16,2,128,128]{3,2,1,0:T(8,128)(2,1)}), bf16[16,2,128,128]{3,2,1,0:T(8,128)(2,1)S(1)}, u32[]{:S(2)}, u32[]{:S(2)}) async-start(bf16[16,2,128,128]{3,2,1,0:T(8,128)(2,1)} %copy.499), calls=%async_computation.6 | async-start | bytes 2097152 | tf_op jit(solution)/shard_map/all_to_all | solution.py:252
  229.0 16.0 %collective-permute-start.5 = (bf16[2,2,128,128]{2,3,0,1:T(8,128)(2,1)}, bf16[2,2,128,128]{2,3,0,1:T(8,128)(2,1)S(1)}, u32[]{:S(2)}, u32[]{:S(2)}) collective-permute-start(bf16[2,2,128,128]{2,3,0,1:T(8,128)(2,1)} %fusion.89), channel_id=1, source_target_pairs={{0,8},{4,12},{8,0},{12,4},{16,24},{20,28},{24,16},{28,20},{1,9},{5... | collective-permute-start | bytes 393224 | tf_op jit(solution)/shard_map/ppermute | solution.py:35
  236.2 27.6 %all-to-all-start = ((bf16[4,128,8,128]{3,2,1,0:T(8,128)(2,1)}), bf16[4,128,8,128]{3,2,1,0:T(8,128)(2,1)}, u32[]{:S(2)}, u32[]{:S(2)}) async-start(bf16[4,128,8,128]{3,2,1,0:T(8,128)(2,1)} %pad_maximum_fusion.4), calls=%async_computation | async-start | bytes 2097152 | tf_op jit(solution)/shard_map/all_to_all | solution.py:64
  241.3 8.3 %collective-permute-start.2 = (bf16[2,128,128]{2,1,0:T(8,128)(2,1)S(1)}, bf16[2,128,128]{2,1,0:T(8,128)(2,1)S(1)}, u32[]{:S(2)}, u32[]{:S(2)}) collective-permute-start(bf16[2,128,128]{2,1,0:T(8,128)(2,1)S(1)} %get-tuple-element.468), channel_id=1, source_target_pairs={{0,4},{4,8},{8,12},{12,16},{16,20},{20,24},{24,28},{1,5},{5,9},{9,... | collective-permute-start | bytes 196616 | tf_op jit(solution)/shard_map/ppermute | solution.py:17
  242.6 7.0 %collective-permute-start.3 = (bf16[2,128,128]{2,1,0:T(8,128)(2,1)S(1)}, bf16[2,128,128]{2,1,0:T(8,128)(2,1)S(1)}, u32[]{:S(2)}, u32[]{:S(2)}) collective-permute-start(bf16[2,128,128]{2,1,0:T(8,128)(2,1)S(1)} %get-tuple-element.469), channel_id=1, source_target_pairs={{4,0},{8,4},{12,8},{16,12},{20,16},{24,20},{28,24},{5,1},{9,5},{13... | collective-permute-start | bytes 196616 | tf_op jit(solution)/shard_map/ppermute | solution.py:18
  245.1 8.1 %collective-permute-start.6 = (bf16[2,2,128,128]{2,3,0,1:T(8,128)(2,1)S(1)}, bf16[2,2,128,128]{2,3,0,1:T(8,128)(2,1)S(1)}, u32[]{:S(2)}, u32[]{:S(2)}) collective-permute-start(bf16[2,2,128,128]{2,3,0,1:T(8,128)(2,1)S(1)} %fusion.99), channel_id=1, source_target_pairs={{0,16},{4,20},{8,24},{12,28},{16,0},{20,4},{24,8},{28,12},{1,17},{... | collective-permute-start | bytes 393224 | tf_op jit(solution)/shard_map/ppermute | solution.py:35
  385.5 19.6 %collective-permute-start.21 = (bf16[128,1,128]{2,0,1:T(8,128)(2,1)}, bf16[128,1,128]{2,0,1:T(8,128)(2,1)}, u32[]{:S(2)}, u32[]{:S(2)}) collective-permute-start(bf16[128,1,128]{2,0,1:T(8,128)(2,1)} %get-tuple-element.493), channel_id=1, source_target_pairs={{0,1},{1,2},{2,3},{3,0},{4,5},{5,6},{6,7},{7,4},{8,9},{9,10},{10,1... | collective-permute-start | bytes 98312 | tf_op jit(solution)/shard_map/ppermute | solution.py:51
  385.5 20.3 %collective-permute-start.22 = (bf16[128,1,128]{2,0,1:T(8,128)(2,1)}, bf16[128,1,128]{2,0,1:T(8,128)(2,1)}, u32[]{:S(2)}, u32[]{:S(2)}) collective-permute-start(bf16[128,1,128]{2,0,1:T(8,128)(2,1)} %get-tuple-element.492), channel_id=1, source_target_pairs={{0,2},{1,3},{2,0},{3,1},{4,6},{5,7},{6,4},{7,5},{8,10},{9,11},{10,... | collective-permute-start | bytes 98312 | tf_op jit(solution)/shard_map/ppermute | solution.py:51
  387.5 19.8 %collective-permute-start.23 = (bf16[128,1,128]{2,0,1:T(8,128)(2,1)}, bf16[128,1,128]{2,0,1:T(8,128)(2,1)}, u32[]{:S(2)}, u32[]{:S(2)}) collective-permute-start(bf16[128,1,128]{2,0,1:T(8,128)(2,1)} %get-tuple-element.491), channel_id=1, source_target_pairs={{0,3},{1,0},{2,1},{3,2},{4,7},{5,4},{6,5},{7,6},{8,11},{9,8},{10,9... | collective-permute-start | bytes 98312 | tf_op jit(solution)/shard_map/ppermute | solution.py:51
  390.0 33.8 %collective-permute-start.26 = (bf16[2,2,128,128]{2,3,0,1:T(8,128)(2,1)}, bf16[2,2,128,128]{2,3,0,1:T(8,128)(2,1)S(1)}, u32[]{:S(2)}, u32[]{:S(2)}) collective-permute-start(bf16[2,2,128,128]{2,3,0,1:T(8,128)(2,1)} %convert_element_type.207), channel_id=1, source_target_pairs={{0,4},{4,0},{8,12},{12,8},{16,20},{20,16},{24,28},{28,24},{1,5},{5... | collective-permute-start | bytes 393224 | tf_op jit(solution)/shard_map/ppermute | solution.py:35
  391.7 24.1 %collective-permute-start.24 = (bf16[2,128,128]{2,1,0:T(8,128)(2,1)}, bf16[2,128,128]{2,1,0:T(8,128)(2,1)}, u32[]{:S(2)}, u32[]{:S(2)}) collective-permute-start(bf16[2,128,128]{2,1,0:T(8,128)(2,1)} %get-tuple-element.466), channel_id=1, source_target_pairs={{0,4},{4,8},{8,12},{12,16},{16,20},{20,24},{24,28},{1,5},{5,9},{9,... | collective-permute-start | bytes 196616 | tf_op jit(solution)/shard_map/ppermute | solution.py:17
  396.8 117.3 %all-to-all-start.9 = ((bf16[16,2,128,128]{3,2,1,0:T(8,128)(2,1)}), bf16[16,2,128,128]{3,2,1,0:T(8,128)(2,1)}, u32[]{:S(2)}, u32[]{:S(2)}) async-start(bf16[16,2,128,128]{3,2,1,0:T(8,128)(2,1)} %copy.524), calls=%async_computation.9 | async-start | bytes 2097152 | tf_op jit(solution)/shard_map/all_to_all | solution.py:252
  405.1 7.0 %collective-permute-start.32 = (bf16[128,1,128]{2,0,1:T(8,128)(2,1)S(1)}, bf16[128,1,128]{2,0,1:T(8,128)(2,1)S(1)}, u32[]{:S(2)}, u32[]{:S(2)}) collective-permute-start(bf16[128,1,128]{2,0,1:T(8,128)(2,1)S(1)} %get-tuple-element.485), channel_id=1, source_target_pairs={{0,1},{1,2},{2,3},{3,0},{4,5},{5,6},{6,7},{7,4},{8,9},{9,10},{10,1... | collective-permute-start | bytes 98312 | tf_op jit(solution)/shard_map/ppermute | solution.py:51
  405.8 7.7 %collective-permute-start.33 = (bf16[128,1,128]{2,0,1:T(8,128)(2,1)S(1)}, bf16[128,1,128]{2,0,1:T(8,128)(2,1)S(1)}, u32[]{:S(2)}, u32[]{:S(2)}) collective-permute-start(bf16[128,1,128]{2,0,1:T(8,128)(2,1)S(1)} %get-tuple-element.484), channel_id=1, source_target_pairs={{0,2},{1,3},{2,0},{3,1},{4,6},{5,7},{6,4},{7,5},{8,10},{9,11},{10,... | collective-permute-start | bytes 98312 | tf_op jit(solution)/shard_map/ppermute | solution.py:51
  407.3 6.3 %collective-permute-start.34 = (bf16[128,1,128]{2,0,1:T(8,128)(2,1)S(1)}, bf16[128,1,128]{2,0,1:T(8,128)(2,1)S(1)}, u32[]{:S(2)}, u32[]{:S(2)}) collective-permute-start(bf16[128,1,128]{2,0,1:T(8,128)(2,1)S(1)} %get-tuple-element.483), channel_id=1, source_target_pairs={{0,3},{1,0},{2,1},{3,2},{4,7},{5,4},{6,5},{7,6},{8,11},{9,8},{10,9... | collective-permute-start | bytes 98312 | tf_op jit(solution)/shard_map/ppermute | solution.py:51
  412.2 6.5 %collective-permute-start.25 = (bf16[2,128,128]{2,1,0:T(8,128)(2,1)S(1)}, bf16[2,128,128]{2,1,0:T(8,128)(2,1)S(1)}, u32[]{:S(2)}, u32[]{:S(2)}) collective-permute-start(bf16[2,128,128]{2,1,0:T(8,128)(2,1)S(1)} %copy-done.16), channel_id=1, source_target_pairs={{4,0},{8,4},{12,8},{16,12},{20,16},{24,20},{28,24},{5,1},{9,5},{13... | collective-permute-start | bytes 196616 | tf_op jit(solution)/shard_map/ppermute | solution.py:18
  413.5 11.8 %collective-permute-start.7 = (bf16[128,8,128]{2,1,0:T(8,128)(2,1)S(1)}, bf16[128,8,128]{2,1,0:T(8,128)(2,1)S(1)}, u32[]{:S(2)}, u32[]{:S(2)}) collective-permute-start(bf16[128,8,128]{2,1,0:T(8,128)(2,1)S(1)} %copy-done.23), channel_id=1, source_target_pairs={{0,1},{1,2},{2,3},{3,0},{4,5},{5,6},{6,7},{7,4},{8,9},{9,10},{10,1... | collective-permute-start | bytes 786440 | tf_op jit(solution)/shard_map/ppermute | solution.py:51
  413.6 20.7 %collective-permute-start.8 = (bf16[128,8,128]{2,1,0:T(8,128)(2,1)S(1)}, bf16[128,8,128]{2,1,0:T(8,128)(2,1)}, u32[]{:S(2)}, u32[]{:S(2)}) collective-permute-start(bf16[128,8,128]{2,1,0:T(8,128)(2,1)S(1)} %copy-done.22), channel_id=1, source_target_pairs={{0,2},{1,3},{2,0},{3,1},{4,6},{5,7},{6,4},{7,5},{8,10},{9,11},{10,... | collective-permute-start | bytes 786440 | tf_op jit(solution)/shard_map/ppermute | solution.py:51
  415.8 21.5 %collective-permute-start.9 = (bf16[128,8,128]{2,1,0:T(8,128)(2,1)S(1)}, bf16[128,8,128]{2,1,0:T(8,128)(2,1)}, u32[]{:S(2)}, u32[]{:S(2)}) collective-permute-start(bf16[128,8,128]{2,1,0:T(8,128)(2,1)S(1)} %copy-done.21), channel_id=1, source_target_pairs={{0,3},{1,0},{2,1},{3,2},{4,7},{5,4},{6,5},{7,6},{8,11},{9,8},{10,9... | collective-permute-start | bytes 786440 | tf_op jit(solution)/shard_map/ppermute | solution.py:51
  418.6 33.2 %collective-permute-start.18 = (bf16[128,8,128]{2,1,0:T(8,128)(2,1)}, bf16[128,8,128]{2,1,0:T(8,128)(2,1)}, u32[]{:S(2)}, u32[]{:S(2)}) collective-permute-start(bf16[128,8,128]{2,1,0:T(8,128)(2,1)} %get-tuple-element.449), channel_id=1, source_target_pairs={{0,1},{1,2},{2,3},{3,0},{4,5},{5,6},{6,7},{7,4},{8,9},{9,10},{10,1... | collective-permute-start | bytes 786440 | tf_op jit(solution)/shard_map/ppermute | solution.py:51
  423.8 44.1 %collective-permute-start.19 = (bf16[128,8,128]{2,1,0:T(8,128)(2,1)}, bf16[128,8,128]{2,1,0:T(8,128)(2,1)S(1)}, u32[]{:S(2)}, u32[]{:S(2)}) collective-permute-start(bf16[128,8,128]{2,1,0:T(8,128)(2,1)} %get-tuple-element.448), channel_id=1, source_target_pairs={{0,2},{1,3},{2,0},{3,1},{4,6},{5,7},{6,4},{7,5},{8,10},{9,11},{10,... | collective-permute-start | bytes 786440 | tf_op jit(solution)/shard_map/ppermute | solution.py:51
  425.3 45.8 %collective-permute-start.20 = (bf16[128,8,128]{2,1,0:T(8,128)(2,1)S(1)}, bf16[128,8,128]{2,1,0:T(8,128)(2,1)S(1)}, u32[]{:S(2)}, u32[]{:S(2)}) collective-permute-start(bf16[128,8,128]{2,1,0:T(8,128)(2,1)S(1)} %get-tuple-element.447), channel_id=1, source_target_pairs={{0,3},{1,0},{2,1},{3,2},{4,7},{5,4},{6,5},{7,6},{8,11},{9,8},{10,9... | collective-permute-start | bytes 786440 | tf_op jit(solution)/shard_map/ppermute | solution.py:51
  434.3 48.5 %collective-permute-start.12 = (bf16[128,8,128]{2,1,0:T(8,128)(2,1)}, bf16[128,8,128]{2,1,0:T(8,128)(2,1)}, u32[]{:S(2)}, u32[]{:S(2)}) collective-permute-start(bf16[128,8,128]{2,1,0:T(8,128)(2,1)} %get-tuple-element.457), channel_id=1, source_target_pairs={{0,1},{1,2},{2,3},{3,0},{4,5},{5,6},{6,7},{7,4},{8,9},{9,10},{10,1... | collective-permute-start | bytes 786440 | tf_op jit(solution)/shard_map/ppermute | solution.py:51
  437.3 51.7 %collective-permute-start.13 = (bf16[128,8,128]{2,1,0:T(8,128)(2,1)}, bf16[128,8,128]{2,1,0:T(8,128)(2,1)}, u32[]{:S(2)}, u32[]{:S(2)}) collective-permute-start(bf16[128,8,128]{2,1,0:T(8,128)(2,1)} %get-tuple-element.456), channel_id=1, source_target_pairs={{0,2},{1,3},{2,0},{3,1},{4,6},{5,7},{6,4},{7,5},{8,10},{9,11},{10,... | collective-permute-start | bytes 786440 | tf_op jit(solution)/shard_map/ppermute | solution.py:51
  451.8 42.5 %collective-permute-start.14 = (bf16[128,8,128]{2,1,0:T(8,128)(2,1)}, bf16[128,8,128]{2,1,0:T(8,128)(2,1)}, u32[]{:S(2)}, u32[]{:S(2)}) collective-permute-start(bf16[128,8,128]{2,1,0:T(8,128)(2,1)} %get-tuple-element.455), channel_id=1, source_target_pairs={{0,3},{1,0},{2,1},{3,2},{4,7},{5,4},{6,5},{7,6},{8,11},{9,8},{10,9... | collective-permute-start | bytes 786440 | tf_op jit(solution)/shard_map/ppermute | solution.py:51
  467.9 30.7 %collective-permute-start.15 = (bf16[128,8,128]{2,1,0:T(8,128)(2,1)}, bf16[128,8,128]{2,1,0:T(8,128)(2,1)}, u32[]{:S(2)}, u32[]{:S(2)}) collective-permute-start(bf16[128,8,128]{2,1,0:T(8,128)(2,1)} %get-tuple-element.445), channel_id=1, source_target_pairs={{0,1},{1,2},{2,3},{3,0},{4,5},{5,6},{6,7},{7,4},{8,9},{9,10},{10,1... | collective-permute-start | bytes 786440 | tf_op jit(solution)/shard_map/ppermute | solution.py:51
  471.1 8.4 %collective-permute-start.27 = (bf16[2,2,128,128]{2,3,0,1:T(8,128)(2,1)}, bf16[2,2,128,128]{2,3,0,1:T(8,128)(2,1)}, u32[]{:S(2)}, u32[]{:S(2)}) collective-permute-start(bf16[2,2,128,128]{2,3,0,1:T(8,128)(2,1)} %fusion.90), channel_id=1, source_target_pairs={{0,8},{4,12},{8,0},{12,4},{16,24},{20,28},{24,16},{28,20},{1,9},{5... | collective-permute-start | bytes 393224 | tf_op jit(solution)/shard_map/ppermute | solution.py:35
  479.5 22.2 %collective-permute-start.16 = (bf16[128,8,128]{2,1,0:T(8,128)(2,1)}, bf16[128,8,128]{2,1,0:T(8,128)(2,1)}, u32[]{:S(2)}, u32[]{:S(2)}) collective-permute-start(bf16[128,8,128]{2,1,0:T(8,128)(2,1)} %get-tuple-element.444), channel_id=1, source_target_pairs={{0,2},{1,3},{2,0},{3,1},{4,6},{5,7},{6,4},{7,5},{8,10},{9,11},{10,... | collective-permute-start | bytes 786440 | tf_op jit(solution)/shard_map/ppermute | solution.py:51
  482.8 18.9 %collective-permute-start.17 = (bf16[128,8,128]{2,1,0:T(8,128)(2,1)}, bf16[128,8,128]{2,1,0:T(8,128)(2,1)}, u32[]{:S(2)}, u32[]{:S(2)}) collective-permute-start(bf16[128,8,128]{2,1,0:T(8,128)(2,1)} %get-tuple-element.443), channel_id=1, source_target_pairs={{0,3},{1,0},{2,1},{3,2},{4,7},{5,4},{6,5},{7,6},{8,11},{9,8},{10,9... | collective-permute-start | bytes 786440 | tf_op jit(solution)/shard_map/ppermute | solution.py:51
  489.0 23.8 %collective-permute-start.28 = (bf16[2,2,128,128]{2,3,0,1:T(8,128)(2,1)}, bf16[2,2,128,128]{2,3,0,1:T(8,128)(2,1)}, u32[]{:S(2)}, u32[]{:S(2)}) collective-permute-start(bf16[2,2,128,128]{2,3,0,1:T(8,128)(2,1)} %fusion.100), channel_id=1, source_target_pairs={{0,16},{4,20},{8,24},{12,28},{16,0},{20,4},{24,8},{28,12},{1,17},{... | collective-permute-start | bytes 393224 | tf_op jit(solution)/shard_map/ppermute | solution.py:35
  516.5 11.3 %collective-permute-start.35 = (bf16[128,1,128]{2,0,1:T(8,128)(2,1)S(1)}, bf16[128,1,128]{2,0,1:T(8,128)(2,1)S(1)}, u32[]{:S(2)}, u32[]{:S(2)}) collective-permute-start(bf16[128,1,128]{2,0,1:T(8,128)(2,1)S(1)} %get-tuple-element.489), channel_id=1, source_target_pairs={{0,1},{1,2},{2,3},{3,0},{4,5},{5,6},{6,7},{7,4},{8,9},{9,10},{10,1... | collective-permute-start | bytes 98312 | tf_op jit(solution)/shard_map/ppermute | solution.py:51
  522.7 6.4 %collective-permute-start.36 = (bf16[128,1,128]{2,0,1:T(8,128)(2,1)S(1)}, bf16[128,1,128]{2,0,1:T(8,128)(2,1)S(1)}, u32[]{:S(2)}, u32[]{:S(2)}) collective-permute-start(bf16[128,1,128]{2,0,1:T(8,128)(2,1)S(1)} %get-tuple-element.488), channel_id=1, source_target_pairs={{0,2},{1,3},{2,0},{3,1},{4,6},{5,7},{6,4},{7,5},{8,10},{9,11},{10,... | collective-permute-start | bytes 98312 | tf_op jit(solution)/shard_map/ppermute | solution.py:51
  523.1 6.0 %collective-permute-start.37 = (bf16[128,1,128]{2,0,1:T(8,128)(2,1)S(1)}, bf16[128,1,128]{2,0,1:T(8,128)(2,1)S(1)}, u32[]{:S(2)}, u32[]{:S(2)}) collective-permute-start(bf16[128,1,128]{2,0,1:T(8,128)(2,1)S(1)} %get-tuple-element.487), channel_id=1, source_target_pairs={{0,3},{1,0},{2,1},{3,2},{4,7},{5,4},{6,5},{7,6},{8,11},{9,8},{10,9... | collective-permute-start | bytes 98312 | tf_op jit(solution)/shard_map/ppermute | solution.py:51
  525.2 6.0 %collective-permute-start.29 = (bf16[128,1,128]{2,0,1:T(8,128)(2,1)S(1)}, bf16[128,1,128]{2,0,1:T(8,128)(2,1)S(1)}, u32[]{:S(2)}, u32[]{:S(2)}) collective-permute-start(bf16[128,1,128]{2,0,1:T(8,128)(2,1)S(1)} %get-tuple-element.497), channel_id=1, source_target_pairs={{0,1},{1,2},{2,3},{3,0},{4,5},{5,6},{6,7},{7,4},{8,9},{9,10},{10,1... | collective-permute-start | bytes 98312 | tf_op jit(solution)/shard_map/ppermute | solution.py:51
  525.3 5.9 %collective-permute-start.30 = (bf16[128,1,128]{2,0,1:T(8,128)(2,1)S(1)}, bf16[128,1,128]{2,0,1:T(8,128)(2,1)S(1)}, u32[]{:S(2)}, u32[]{:S(2)}) collective-permute-start(bf16[128,1,128]{2,0,1:T(8,128)(2,1)S(1)} %get-tuple-element.496), channel_id=1, source_target_pairs={{0,2},{1,3},{2,0},{3,1},{4,6},{5,7},{6,4},{7,5},{8,10},{9,11},{10,... | collective-permute-start | bytes 98312 | tf_op jit(solution)/shard_map/ppermute | solution.py:51
  527.8 3.9 collective-permute-start.31
  (80 other events, 642.8 us)
Sparse Core Ops, SparseCore 0:
  31.8 26.8 all-gather.2
  61.1 27.9 all-gather.4
